TPU v7x, 32 devices: a whole 2x2x4 slice. The times are simulated.
32 devices in a mesh: pair: 4 (over z), gen: 8 (over y, x, core).
Axes of the slice: x: 2, y: 2, z: 4, core: 2. Of those that a mesh axis runs over, the one named last changes fastest.
Arguments:
- tokens: bfloat16 [32768, 2048], P(('pair', 'gen')), may hold values from -6 to 6
- cotangent: bfloat16 [32768, 256], P(('pair', 'gen')), may hold values from -6 to 6
- block_pair: int32 [32, 1], replicated, may hold values from 0 to 15
- src_lang: int32 [16], replicated, may hold values from 0 to 95
- tgt_lang: int32 [16], replicated, may hold values from 0 to 95
- lang_embed: float32 [96, 512], P(None, 'pair'), may hold values from -5 to 5
- generator: bfloat16 [512, 524288], P('pair', 'gen'), may hold values from -0.005859375 to 0.005859375
Outputs:
- grad_tokens: bfloat16 [32768, 2048], P(('pair', 'gen'))
- grad_generator: bfloat16 [512, 524288], P('pair', 'gen')
- grad_embed: float32 [96, 512], P(None, 'pair')
Inputs may be any that keep to these rules, and one draw needn't show every extreme that they name: `block_pair`: every pair owns at least one block; block counts per pair are uneven.
All inputs are finite; a program needn't handle non-finite values.
Results may differ from a plain program's by a relative error of at most 0.007.
Values may be sent and summed in bfloat16 or wider, within the bound.
No kernel may reach another device: no remote copies, remote signals or barrier semaphores. Data moves between devices by JAX's collectives and lax.ppermute only.
A program may use at most 128 MiB of HBM per device.

v0:
```python
import jax
import jax.numpy as jnp
from jax import lax
from jax.sharding import PartitionSpec as P

BLK = 1024


def shards(tokens, cotangent, block_pair, src_lang, tgt_lang, lang_embed, generator):
    gen_count = lax.axis_size("gen")
    pair_index = lax.axis_index("pair")
    blocks_here = tokens.shape[0] // BLK
    model_width = tokens.shape[1]
    adapter_rank = cotangent.shape[1]
    languages = lang_embed.shape[0]
    pair_count = src_lang.shape[0]
    lang_ids = jnp.arange(languages, dtype=jnp.int32)
    hot_both = (src_lang[:, None] == lang_ids[None, :]).astype(jnp.float32) + (
        tgt_lang[:, None] == lang_ids[None, :]
    ).astype(jnp.float32)
    pair_embed = jnp.dot(hot_both, lang_embed, precision=lax.Precision.HIGHEST).astype(jnp.bfloat16)
    partial_value = jnp.dot(pair_embed, generator, preferred_element_type=jnp.float32)
    adapter_cols = lax.psum(partial_value, "pair").astype(jnp.bfloat16)
    flat_pairs = block_pair[:, 0]
    row_pairs = lax.dynamic_slice_in_dim(
        flat_pairs, pair_index * (gen_count * blocks_here), gen_count * blocks_here
    )
    send_order = row_pairs.reshape(gen_count, blocks_here).T
    outgoing = jnp.take(adapter_cols, send_order, axis=0).reshape(
        blocks_here, gen_count * adapter_cols.shape[1]
    )
    own_adapters = lax.all_to_all(outgoing, "gen", split_axis=1, concat_axis=1, tiled=True)
    adapters = own_adapters.reshape(blocks_here, model_width, adapter_rank)
    token_blocks = tokens.reshape(blocks_here, BLK, model_width)
    cot_blocks = cotangent.reshape(blocks_here, BLK, adapter_rank)
    hidden = jnp.einsum("btd,bdr->btr", token_blocks, adapters, preferred_element_type=jnp.float32)
    logistic = jax.nn.sigmoid(hidden)
    grad_hidden = (
        cot_blocks.astype(jnp.float32) * logistic * (1.0 + hidden * (1.0 - logistic))
    ).astype(jnp.bfloat16)
    grad_tokens = (
        jnp.einsum("btr,bdr->btd", grad_hidden, adapters, preferred_element_type=jnp.float32)
        .astype(jnp.bfloat16)
        .reshape(tokens.shape)
    )
    outer_grads = jnp.einsum(
        "btd,btr->bdr", token_blocks, grad_hidden, preferred_element_type=jnp.float32
    ).reshape(blocks_here, model_width * adapter_rank)
    returned = lax.all_to_all(outer_grads, "gen", split_axis=1, concat_axis=0, tiled=True)
    pair_ids = jnp.arange(pair_count, dtype=jnp.int32)
    segment_hot = (pair_ids[:, None] == row_pairs[None, :]).astype(jnp.float32)
    row_grad = jnp.dot(segment_hot, returned, precision=lax.Precision.HIGHEST)
    grad_rounded = lax.psum(row_grad, "pair").astype(jnp.bfloat16)
    grad_generator = jnp.einsum(
        "pe,pc->ec", pair_embed, grad_rounded, preferred_element_type=jnp.float32
    ).astype(jnp.bfloat16)
    partial_pair = jnp.einsum(
        "pc,ec->pe", grad_rounded, generator, preferred_element_type=jnp.float32
    )
    grad_pair = lax.psum(partial_pair, "gen")
    grad_embed = jnp.dot(hot_both.T, grad_pair, precision=lax.Precision.HIGHEST)
    return (grad_tokens, grad_generator, grad_embed)


def solution(mesh):
    placed = (
        P(("pair", "gen"), None),
        P(("pair", "gen"), None),
        P(),
        P(),
        P(),
        P(None, "pair"),
        P("pair", "gen"),
    )
    return jax.shard_map(
        shards,
        mesh=mesh,
        in_specs=placed,
        out_specs=(P(("pair", "gen"), None), P("pair", "gen"), P(None, "pair")),
        check_vma=False,
    )
```

profile of v0, /device:TPU:0, one launch (start us, length us, event | category | flops | bytes accessed | tf_op | source)
XLA Modules:
  0.0 421.6 jit_solution(15591775119214140472)
XLA Ops:
  0.6 0.0 copy-start
  0.7 0.7 fusion.16
  1.4 0.7 compare_and_fusion
  2.1 0.9 convolution_convert_fusion.2
  3.0 10.1 %fusion.21 = f32[16,65536]{1,0:T(8,128)} fusion(bf16[16,128]{1,0:T(8,128)(2,1)S(1)} %convolution_convert_fusion.2, bf16[128,65536]{1,0:T(8,128)(2,1)} %param.13), kind=kOutput, calls=%fused_computation.39 | convolution fusion | flops 268435456 | bytes 20975616 | tf_op jit(solution)/shard_map/dot_general | solution.py:22
  13.1 149.0 %all-reduce.2 = bf16[16,65536]{1,0:T(8,128)(2,1)S(1)} all-reduce(f32[16,65536]{1,0:T(8,128)} %fusion.21), channel_id=1, replica_groups=mesh['pair'=4,'gen'=8] {'pair'}, use_global_device_ids=true, to_apply=%region_0.0 | all-reduce | flops 1048576 | bytes 6291456 | tf_op jit(solution)/shard_map/psum | solution.py:23
  162.1 1.2 gather_fusion
  163.4 0.2 bitcast_select_fusion
  163.5 1.6 copy.27
  165.2 0.5 broadcast.100
  165.7 7.0 %reduce.2 = bf16[8,65536]{1,0:T(8,128)(2,1)S(1)} reduce(bf16[8,1,65536]{2,1,0:T(2,128)(2,1)S(1)} %bitcast.33, bf16[]{:T(256)} %broadcast.100), dimensions={1}, to_apply=%bitcast.32.reduce_sub_computation | reduce | bytes 2097154
  172.7 1.9 reshape.166
  174.6 3.8 all-to-all-start
  178.4 1.0 copy.17
  179.4 14.3 %all-to-all-done = bf16[8,2,32768]{2,1,0:T(2,128)(2,1)S(1)} async-done(((bf16[8,2,32768]{2,1,0:T(2,128)(2,1)}), bf16[8,2,32768]{2,1,0:T(2,128)(2,1)S(1)}, u32[]{:S(2)}, u32[]{:S(2)}) %all-to-all-start) | async-done | bytes 1048608 | tf_op jit(solution)/shard_map/all_to_all | solution.py:32
  193.7 1.0 reshape.167
  194.8 6.0 %bitcast_reduce_fusion = bf16[8,65536]{1,0:T(8,128)(2,1)S(1)} fusion(bf16[8,1,65536]{2,1,0:T(2,128)(2,1)S(1)} %reshape.167), kind=kLoop, calls=%fused_computation.37 | loop fusion | bytes 2097152 | tf_op jit(solution)/shard_map/all_to_all | solution.py:32
  200.8 0.5 reshape.156
  201.3 3.9 convolution_bitcast_fusion.1
  205.2 1.0 copy-done.9
  206.2 2.9 convolution_bitcast_fusion
  209.1 1.9 copy.19
  211.0 4.2 all_to_all.20
  215.2 3.9 all-to-all-start.1
  219.0 5.0 %convolution_convert_fusion.1 = bf16[1024,2048]{1,0:T(8,128)(2,1)} fusion(bf16[2048,256]{1,0:T(8,128)(2,1)S(1)} %copy-done.3, f32[1024,256]{0,1:T(8,128)} %copy-done.9, bf16[1024,256]{0,1:T(8,128)(2,1)} %copy.17), kind=kOutput, calls=%fused_computation.2 | convolution fusion | flops 1078460416 | bytes 6815744 | tf_op jit(solution)/shard_map/btr,bdr->btd/dot_general | solution.py:42
  224.0 21.3 %all-to-all-done.1 = f32[1,8,65536]{2,0,1:T(1,128)S(1)} async-done(((f32[1,8,65536]{2,0,1:T(1,128)}), f32[1,8,65536]{2,0,1:T(1,128)S(1)}, u32[]{:S(2)}, u32[]{:S(2)}) %all-to-all-start.1) | async-done | bytes 2097184 | tf_op jit(solution)/shard_map/all_to_all | solution.py:49
  245.3 4.8 %fusion = f32[16,65536]{1,0:T(8,128)} fusion(f32[1,8,65536]{2,0,1:T(1,128)S(1)} %all-to-all-done.1, s32[8]{0:T(128)S(1)} %get-tuple-element.4), kind=kOutput, calls=%fused_computation.4 | convolution fusion | flops 100663424 | bytes 6291488 | tf_op jit(solution)/shard_map/dot_general | solution.py:52
  250.1 141.2 %all-reduce.3 = bf16[16,65536]{1,0:T(8,128)(2,1)S(1)} all-reduce(f32[16,65536]{1,0:T(8,128)} %fusion), channel_id=1, replica_groups=mesh['pair'=4,'gen'=8] {'pair'}, use_global_device_ids=true, to_apply=%region_1.2 | all-reduce | flops 1048576 | bytes 6291456 | tf_op jit(solution)/shard_map/psum | solution.py:53
  391.4 8.5 %convolution_convert_fusion = bf16[128,65536]{1,0:T(8,128)(2,1)} fusion(bf16[16,128]{1,0:T(8,128)(2,1)S(1)} %convolution_convert_fusion.2, bf16[16,65536]{1,0:T(8,128)(2,1)S(1)} %all-reduce.3), kind=kOutput, calls=%fused_computation.1 | convolution fusion | flops 276824064 | bytes 18878464 | tf_op jit(solution)/shard_map/pe,pc->ec/dot_general | solution.py:54
  399.9 8.1 %fusion.22 = f32[16,128]{1,0:T(8,128)S(1)} fusion(bf16[16,65536]{1,0:T(8,128)(2,1)S(1)} %all-reduce.3, bf16[128,65536]{1,0:T(8,128)(2,1)} %param.13), kind=kOutput, calls=%fused_computation.40 | convolution fusion | flops 268435456 | bytes 18882560 | tf_op jit(solution)/shard_map/pc,ec->pe/dot_general | solution.py:57
  408.0 12.6 %psum.23 = f32[16,128]{1,0:T(8,128)S(1)} all-reduce(f32[16,128]{1,0:T(8,128)S(1)} %fusion.22), channel_id=1, replica_groups=mesh['pair'=4,'gen'=8] {'gen'}, use_global_device_ids=true, to_apply=%region_2.3 | all-reduce | flops 2048 | bytes 16384 | tf_op jit(solution)/shard_map/psum | solution.py:60
  420.6 1.0 fusion.10
  (19 shorter events, 0.0 us)
Async XLA Ops:
  0.6 1.5 copy-start
  172.7 5.7 %copy-start.4 = (bf16[1024,256]{1,0:T(8,128)(2,1)S(1)}, bf16[1024,256]{1,0:T(8,128)(2,1)}, u32[]{:S(2)}) copy-start(bf16[1024,256]{1,0:T(8,128)(2,1)} %param.8) | copy-start | bytes 1572868
  174.6 19.1 %all-to-all-start = ((bf16[8,2,32768]{2,1,0:T(2,128)(2,1)}), bf16[8,2,32768]{2,1,0:T(2,128)(2,1)S(1)}, u32[]{:S(2)}, u32[]{:S(2)}) async-start(bf16[8,2,32768]{2,1,0:T(2,128)(2,1)} %reshape.166), calls=%async_computation | async-start | bytes 2097152 | tf_op jit(solution)/shard_map/all_to_all | solution.py:32
  201.3 3.9 copy-start.2
  201.3 4.9 %copy-start.5 = (bf16[1024,256]{0,1:T(8,128)(2,1)S(1)}, bf16[1024,256]{0,1:T(8,128)(2,1)}, u32[]{:S(2)}) copy-start(bf16[1024,256]{0,1:T(8,128)(2,1)} %copy.17) | copy-start | bytes 1572868
  201.3 4.9 %copy-start.6 = (bf16[1024,2048]{1,0:T(8,128)(2,1)S(1)}, bf16[1024,2048]{1,0:T(8,128)(2,1)}, u32[]{:S(2)}) copy-start(bf16[1024,2048]{1,0:T(8,128)(2,1)} %param.7) | copy-start | bytes 12582916
  205.2 1.0 copy-start.9
  211.0 8.0 %copy-start.3 = (bf16[2048,256]{1,0:T(8,128)(2,1)S(1)}, bf16[2048,256]{1,0:T(8,128)(2,1)}, u32[]{:S(2)}) copy-start(bf16[2048,256]{1,0:T(8,128)(2,1)} %copy-done.2) | copy-start | bytes 3145732
  215.2 30.2 %all-to-all-start.1 = ((f32[1,8,65536]{2,0,1:T(1,128)}), f32[1,8,65536]{2,0,1:T(1,128)S(1)}, u32[]{:S(2)}, u32[]{:S(2)}) async-start(f32[1,8,65536]{2,0,1:T(1,128)} %all_to_all.20), calls=%async_computation.1 | async-start | bytes 4194304 | tf_op jit(solution)/shard_map/all_to_all | solution.py:49
  399.9 20.7 %copy-start.7 = (s32[16]{0:T(128)S(1)}, s32[16]{0:T(128)}, u32[]{:S(2)}) copy-start(s32[16]{0:T(128)} %param.11) | copy-start | bytes 196
  399.9 20.7 %copy-start.8 = (s32[16]{0:T(128)S(1)}, s32[16]{0:T(128)}, u32[]{:S(2)}) copy-start(s32[16]{0:T(128)} %param.10) | copy-start | bytes 196
  399.9 21.7 %copy-start.1 = (f32[96,128]{1,0:T(8,128)S(1)}, f32[96,128]{1,0:T(8,128)}, u32[]{:S(2)}) copy-start(f32[96,128]{1,0:T(8,128)} %param.12) | copy-start | bytes 147460
where the time goes:
time: 422 us
  blocking collectives  303 us (72%)
  matrix products  45.1 us (11%)
  waiting for transfers between devices  35.7 us (8%)
  local copies, waits for them, and re-layouts  20.8 us (5%)
  other arithmetic  8.67 us (2%)
  starting transfers between devices  7.64 us (2%)
    psum x1, blocking collectives, shards(): adapter_cols = lax.psum(partial_value, 'pair').astype(jnp.bfloat16)  149 us
    psum x1, blocking collectives, shards(): grad_rounded = lax.psum(row_grad, 'pair').astype(jnp.bfloat16)  141 us
    all_to_all x1, waiting for transfers between devices, shards(): lax.all_to_all(outer_grads, 'gen', split_axis=1, concat_axis=0, tiled=True)  21.3 us
    all_to_all x1, waiting for transfers between devices, shards(): lax.all_to_all(outgoing, 'gen', split_axis=1, concat_axis=1, tiled=True)  14.3 us
    psum x1, blocking collectives, shards(): grad_pair = lax.psum(partial_pair, 'gen')  12.6 us
    dot_general x1, matrix products, shards(): jnp.dot(pair_embed, generator, preferred_element_type=jnp.float32)  10.1 us
    dot_general x1, matrix products, shards(): jnp.einsum('pe,pc->ec', pair_embed, grad_rounded, preferred_element_type=...  8.55 us
  transfers between devices with their start and end apart: 2, of which 2 were waited for; matrix products, arithmetic and copies ran while one was open for 1% of the time, Pallas kernels for 0%

commit v1 on v0

--- a/solution.py
+++ b/solution.py
@@ -1,9 +1,19 @@
+import functools
 import jax
 import jax.numpy as jnp
 from jax import lax
 from jax.sharding import PartitionSpec as P
 
 BLK = 1024
+
+
+def wrap_stops_all(x0, peer_axis):
+    main = lax.all_gather(x0, peer_axis)
+    s_next = jnp.sum(main, axis=0)
+    return s_next
+
+
+_close_threads = functools.partial(wrap_stops_all, peer_axis="pair")
 
 
 def shards(tokens, cotangent, block_pair, src_lang, tgt_lang, lang_embed, generator):
@@ -20,7 +30,7 @@
     ).astype(jnp.float32)
     pair_embed = jnp.dot(hot_both, lang_embed, precision=lax.Precision.HIGHEST).astype(jnp.bfloat16)
     partial_value = jnp.dot(pair_embed, generator, preferred_element_type=jnp.float32)
-    adapter_cols = lax.psum(partial_value, "pair").astype(jnp.bfloat16)
+    adapter_cols = _close_threads(partial_value).astype(jnp.bfloat16)
     flat_pairs = block_pair[:, 0]
     row_pairs = lax.dynamic_slice_in_dim(
         flat_pairs, pair_index * (gen_count * blocks_here), gen_count * blocks_here

time: 422 us -> 583 us (1.38)
  waiting for transfers between devices: 35.7 us -> 325 us
  blocking collectives: 303 us -> 154 us
  between operations: 0.86 us -> 14.2 us
  other arithmetic: 8.67 us -> 15.1 us
    all_gather x0 -> x1, waiting for transfers between devices: none -> 289 us  [wrap_stops_all(): main = lax.all_gather(x0, peer_axis)]
    psum x1 -> x0, blocking collectives: 149 us -> none  [shards(): adapter_cols = lax.psum(partial_value, 'pair').astype(jnp.bfloat16)]
    reduce_sum x0 -> x1, other arithmetic: none -> 7.57 us  [wrap_stops_all(): s_next = jnp.sum(main, axis=0)]
  transfers between devices with their start and end apart: 2 -> 3, of which waited for: 2 -> 3; matrix products, arithmetic and copies ran while one was open for 1% -> 1% of each run, Pallas kernels for 0% -> 0%
where the time goes in v1:
time: 583 us
  waiting for transfers between devices  325 us (56%)
  blocking collectives  154 us (26%)
  matrix products  45 us (8%)
  local copies, waits for them, and re-layouts  22.2 us (4%)
  other arithmetic  15.1 us (3%)
  between operations  14.2 us (2%)
  starting transfers between devices  7.52 us (1%)
    all_gather x1, waiting for transfers between devices, wrap_stops_all(): main = lax.all_gather(x0, peer_axis)  289 us
    psum x1, blocking collectives, shards(): grad_rounded = lax.psum(row_grad, 'pair').astype(jnp.bfloat16)  141 us
    all_to_all x1, waiting for transfers between devices, shards(): lax.all_to_all(outer_grads, 'gen', split_axis=1, concat_axis=0, tiled=True)  21.4 us
    all_to_all x1, waiting for transfers between devices, shards(): lax.all_to_all(outgoing, 'gen', split_axis=1, concat_axis=1, tiled=True)  14.4 us
    psum x1, blocking collectives, shards(): grad_pair = lax.psum(partial_pair, 'gen')  12.6 us
  transfers between devices with their start and end apart: 3, of which 3 were waited for; matrix products, arithmetic and copies ran while one was open for 1% of the time, Pallas kernels for 0%

profile of v1, /device:TPU:0, one launch (start us, length us, event | category | flops | bytes accessed | tf_op | source)
XLA Modules:
  0.0 582.6 jit_solution(9602623355460629875)
XLA Ops:
  7.2 0.7 copy-done
  8.0 0.9 convolution_convert_fusion.2
  8.8 10.1 %fusion.21 = f32[16,65536]{1,0:T(8,128)} fusion(bf16[16,128]{1,0:T(8,128)(2,1)S(1)} %convolution_convert_fusion.2, bf16[128,65536]{1,0:T(8,128)(2,1)} %param.13), kind=kOutput, calls=%fused_computation.39 | convolution fusion | flops 268435456 | bytes 20975616 | tf_op jit(solution)/shard_map/dot_general | solution.py:32
  19.0 0.6 copy-done.6
  19.8 288.8 %all-gather.3.cloned.1.call-done = f32[64,65536]{1,0:T(8,128)} async-done(((f32[16,65536]{1,0:T(8,128)}), f32[64,65536]{1,0:T(8,128)}) %all-gather.3.cloned.1.call-update) | async-done | bytes 16777232 | tf_op jit(solution)/shard_map/all_gather | solution.py:11
  308.6 7.6 %reduce_sum.9 = bf16[16,65536]{1,0:T(8,128)(2,1)S(1)} reduce(f32[4,16,65536]{2,1,0:T(8,128)} %bitcast.34, f32[]{:T(128)} %constant.29.clone.1), dimensions={0}, to_apply=%region_0.0 | reduce | flops 3145728 | bytes 18874372 | tf_op jit(solution)/shard_map/reduce_sum | solution.py:12
  316.2 1.2 gather_fusion
  317.4 0.2 bitcast_select_fusion
  317.6 1.6 copy.27
  319.2 0.5 broadcast.100
  319.7 7.2 %reduce.2 = bf16[8,65536]{1,0:T(8,128)(2,1)S(1)} reduce(bf16[8,1,65536]{2,1,0:T(2,128)(2,1)S(1)} %bitcast.35, bf16[]{:T(256)} %broadcast.100), dimensions={1}, to_apply=%bitcast.33.reduce_sub_computation | reduce | bytes 2097154
  327.0 1.9 reshape.167
  328.8 3.7 all-to-all-start
  332.5 1.0 copy.17
  333.5 14.4 %all-to-all-done = bf16[8,2,32768]{2,1,0:T(2,128)(2,1)S(1)} async-done(((bf16[8,2,32768]{2,1,0:T(2,128)(2,1)}), bf16[8,2,32768]{2,1,0:T(2,128)(2,1)S(1)}, u32[]{:S(2)}, u32[]{:S(2)}) %all-to-all-start) | async-done | bytes 1048608 | tf_op jit(solution)/shard_map/all_to_all | solution.py:42
  347.9 1.0 reshape.168
  348.9 6.0 %bitcast_reduce_fusion = bf16[8,65536]{1,0:T(8,128)(2,1)S(1)} fusion(bf16[8,1,65536]{2,1,0:T(2,128)(2,1)S(1)} %reshape.168), kind=kLoop, calls=%fused_computation.37 | loop fusion | bytes 2097152 | tf_op jit(solution)/shard_map/all_to_all | solution.py:42
  354.9 0.5 reshape.156
  355.5 3.9 convolution_bitcast_fusion.1
  359.4 1.0 copy-done.10
  360.3 2.9 convolution_bitcast_fusion
  363.2 1.9 copy.19
  365.1 4.2 all_to_all.20
  369.3 3.8 all-to-all-start.1
  373.1 5.0 convolution_convert_fusion.1
  378.1 21.4 %all-to-all-done.1 = f32[1,8,65536]{2,0,1:T(1,128)S(1)} async-done(((f32[1,8,65536]{2,0,1:T(1,128)}), f32[1,8,65536]{2,0,1:T(1,128)S(1)}, u32[]{:S(2)}, u32[]{:S(2)}) %all-to-all-start.1) | async-done | bytes 2097184 | tf_op jit(solution)/shard_map/all_to_all | solution.py:59
  399.5 4.8 fusion
  404.3 141.2 %all-reduce.1 = bf16[16,65536]{1,0:T(8,128)(2,1)S(1)} all-reduce(f32[16,65536]{1,0:T(8,128)} %fusion), channel_id=1, replica_groups=mesh['pair'=4,'gen'=8] {'pair'}, use_global_device_ids=true, to_apply=%region_1.2 | all-reduce | flops 1048576 | bytes 6291456 | tf_op jit(solution)/shard_map/psum | solution.py:63
  545.5 8.5 %convolution_convert_fusion = bf16[128,65536]{1,0:T(8,128)(2,1)} fusion(bf16[16,128]{1,0:T(8,128)(2,1)S(1)} %convolution_convert_fusion.2, bf16[16,65536]{1,0:T(8,128)(2,1)S(1)} %all-reduce.1), kind=kOutput, calls=%fused_computation.1 | convolution fusion | flops 276824064 | bytes 18878464 | tf_op jit(solution)/shard_map/pe,pc->ec/dot_general | solution.py:64
  554.1 8.1 %fusion.22 = f32[16,128]{1,0:T(8,128)S(1)} fusion(bf16[16,65536]{1,0:T(8,128)(2,1)S(1)} %all-reduce.1, bf16[128,65536]{1,0:T(8,128)(2,1)} %param.13), kind=kOutput, calls=%fused_computation.40 | convolution fusion | flops 268435456 | bytes 18882560 | tf_op jit(solution)/shard_map/pc,ec->pe/dot_general | solution.py:67
  562.1 12.6 %psum.15 = f32[16,128]{1,0:T(8,128)S(1)} all-reduce(f32[16,128]{1,0:T(8,128)S(1)} %fusion.22), channel_id=1, replica_groups=mesh['pair'=4,'gen'=8] {'gen'}, use_global_device_ids=true, to_apply=%region_2.3 | all-reduce | flops 2048 | bytes 16384 | tf_op jit(solution)/shard_map/psum | solution.py:70
  574.8 1.0 fusion.10
  (24 shorter events, 0.3 us)
Async XLA Ops:
  7.2 0.8 copy-start
  7.2 301.4 %all-gather.3.cloned.1.call-start = ((), (), s32[]{:S(2)}) async-start(), calls=%async_computation.2 | async-start | bytes 20971520 | tf_op jit(solution)/shard_map/all_gather | solution.py:11
  18.9 0.7 copy-start.6
  327.0 5.5 copy-start.4
  328.8 19.1 %all-to-all-start = ((bf16[8,2,32768]{2,1,0:T(2,128)(2,1)}), bf16[8,2,32768]{2,1,0:T(2,128)(2,1)S(1)}, u32[]{:S(2)}, u32[]{:S(2)}) async-start(bf16[8,2,32768]{2,1,0:T(2,128)(2,1)} %reshape.167), calls=%async_computation | async-start | bytes 2097152 | tf_op jit(solution)/shard_map/all_to_all | solution.py:42
  355.4 3.9 copy-start.2
  355.4 4.9 copy-start.5
  355.4 4.9 copy-start.7
  359.4 1.0 copy-start.10
  365.1 8.0 %copy-start.3 = (bf16[2048,256]{1,0:T(8,128)(2,1)S(1)}, bf16[2048,256]{1,0:T(8,128)(2,1)}, u32[]{:S(2)}) copy-start(bf16[2048,256]{1,0:T(8,128)(2,1)} %copy-done.2) | copy-start | bytes 3145732
  369.3 30.2 %all-to-all-start.1 = ((f32[1,8,65536]{2,0,1:T(1,128)}), f32[1,8,65536]{2,0,1:T(1,128)S(1)}, u32[]{:S(2)}, u32[]{:S(2)}) async-start(f32[1,8,65536]{2,0,1:T(1,128)} %all_to_all.20), calls=%async_computation.1 | async-start | bytes 4194304 | tf_op jit(solution)/shard_map/all_to_all | solution.py:59
  554.1 20.7 %copy-start.8 = (s32[16]{0:T(128)S(1)}, s32[16]{0:T(128)}, u32[]{:S(2)}) copy-start(s32[16]{0:T(128)} %param.11) | copy-start | bytes 196
  554.1 20.7 %copy-start.9 = (s32[16]{0:T(128)S(1)}, s32[16]{0:T(128)}, u32[]{:S(2)}) copy-start(s32[16]{0:T(128)} %param.10) | copy-start | bytes 196
  554.1 21.7 %copy-start.1 = (f32[96,128]{1,0:T(8,128)S(1)}, f32[96,128]{1,0:T(8,128)}, u32[]{:S(2)}) copy-start(f32[96,128]{1,0:T(8,128)} %param.12) | copy-start | bytes 147460
Sparse Core Ops, SparseCore 0:
  19.1 289.4 all-gather.2
